TPU v7x, 32 devices: a whole 2x2x4 slice. The times are simulated.
32 devices in a mesh: grp: 2 (over y), row: 8 (over z, x), chan: 2 (over core).
Axes of the slice: x: 2, y: 2, z: 4, core: 2. Of those that a mesh axis runs over, the one named last changes fastest.
Arguments:
- band_strip: bfloat16 [424, 64, 128], P('chan', ('grp', 'row')), parts along dimension 1, may hold values from -6 to 6
- conv_weight: bfloat16 [1024, 9, 424], P('row', None, 'chan'), may hold values from -0.09375 to 0.09375
- gdn_gamma: bfloat16 [1024, 1024], P('chan'), as said below
- gdn_beta: float32 [1024], P('chan'), may hold values from 0.5 to 2
- cotangent: bfloat16 [1024, 64, 128], P('chan', ('grp', 'row')), parts along dimension 1, may hold values from -6 to 6
Outputs:
- latent: bfloat16 [1024, 64, 128], P('chan', ('grp', 'row')), parts along dimension 1
- grad_strip: float32 [424, 64, 128], P('chan', ('grp', 'row')), parts along dimension 1
- grad_gamma: float32 [2048, 1024], P(('grp', 'chan')), parts along dimension 0
- grad_beta: float32 [2048], P(('grp', 'chan')), parts along dimension 0
There are 2 independent parts, one for each index of `grp`. A program takes and returns all parts, laid end to end along the dimension named above; an argument that names none is the same for every part. Nothing has to cross between parts.
Inputs may be any that keep to these rules, and one draw needn't show every extreme that they name: `gdn_gamma`: gamma's entries are non-negative.
All inputs are finite; a program needn't handle non-finite values.
Results may differ from a plain program's by a relative error of at most 0.0054.
Values may be sent and summed in bfloat16 or wider, within the bound.
No kernel may reach another device: no remote copies, remote signals or barrier semaphores. Data moves between devices by JAX's collectives and lax.ppermute only.
A program may use at most 64 MiB of HBM per device.

v0:
```python
import math
import jax
import jax.numpy as jnp
from jax import lax
from jax.sharding import PartitionSpec as P

TAPS = ((-1, -1), (-1, 0), (-1, 1), (0, -1), (0, 0), (0, 1), (1, -1), (1, 0), (1, 1))
SWAP = [(0, 1), (1, 0)]


def extended(shard, sides, width):
    for axis, dim in sides:
        count, length = (lax.axis_size(axis), shard.shape[dim])
        up = [(i, (i + 1) % count) for i in range(count - 1)]
        down = [(j, i) for i, j in up]
        last = lax.slice_in_dim(shard, length - width, length, axis=dim)
        leading = lax.slice_in_dim(shard, 0, width, axis=dim)
        before = lax.ppermute(last, axis, up)
        after = lax.ppermute(leading, axis, down)
        shard = jnp.concatenate([before, shard, after], axis=dim)
    return shard


def tap_columns(rimmed, row_count, col_count):
    padded = jnp.pad(rimmed, ((0, 0), (0, 0), (1, 1)))
    stacked = jnp.stack(
        [
            padded[
                :,
                1 + row_shift : 1 + row_shift + row_count,
                1 + col_shift : 1 + col_shift + col_count,
            ]
            for row_shift, col_shift in TAPS
        ],
        axis=0,
    )
    return stacked.reshape(9 * rimmed.shape[0], row_count * col_count)


def chan_gather(x):
    other = lax.ppermute(x, "chan", SWAP)
    first = lax.axis_index("chan") == 0
    return jnp.where(first, jnp.concatenate([x, other], 0), jnp.concatenate([other, x], 0))


def chan_scatter_sum(x):
    half = x.shape[0] // 2
    first = lax.axis_index("chan") == 0
    top, bottom = (x[:half], x[half:])
    mine = jnp.where(first, top, bottom)
    theirs = jnp.where(first, bottom, top)
    return mine + lax.ppermute(theirs, "chan", SWAP)


def ring_order(mesh):
    count = mesh.shape["row"]
    try:
        coords = [tuple(d.coords) for d in mesh.devices[0, :, 0]]
    except Exception:
        return list(range(count))
    xs = sorted({c[0] for c in coords})
    zs = sorted({c[2] for c in coords})
    if len(xs) * len(zs) != count or len(zs) % 2:
        return list(range(count))
    where = {(c[0], c[2]): i for i, c in enumerate(coords)}
    path = [where[xs[0], zs[0]]]
    for k, z in enumerate(zs):
        cols = xs[1:] if k % 2 == 0 else xs[:0:-1]
        path += [where[x, z] for x in cols]
    path += [where[xs[0], z] for z in zs[:0:-1]]
    return path if len(set(path)) == count else list(range(count))


def ring_sum(blocks, ring):
    count = len(ring)
    forward = [(ring[i], ring[(i + 1) % count]) for i in range(count)]
    backward = [(b, a) for a, b in forward]
    position = jnp.asarray([ring.index(i) for i in range(count)], jnp.int32)[lax.axis_index("row")]

    def chunks(x, part):
        half = x.shape[0] // 2
        piece = x[part * half : (part + 1) * half]
        return piece.reshape((count, half // count) + x.shape[1:])

    split = [[chunks(x, part) for x in blocks] for part in range(2)]
    moves = (forward, backward)
    signs = (1, -1)

    def pick(part, step):
        index = (position - signs[part] * (1 + step)) % count
        return [jnp.take(c, index, axis=0) for c in split[part]]

    carry = [pick(part, 0) for part in range(2)]
    for step in range(1, count):
        for part in range(2):
            got = lax.ppermute(carry[part], "row", moves[part])
            carry[part] = [g + o for g, o in zip(got, pick(part, step))]
    gathered = [[c] for c in carry]
    for step in range(1, count):
        for part in range(2):
            gathered[part].append(lax.ppermute(gathered[part][-1], "row", moves[part]))
    results = []
    for leaf in range(len(blocks)):
        halves = []
        for part in range(2):
            stacked = jnp.stack([g[leaf] for g in gathered[part]], 0)
            order = signs[part] * (position - jnp.arange(count)) % count
            halves.append(jnp.take(stacked, order, axis=0).reshape((-1,) + stacked.shape[2:]))
        results.append(jnp.concatenate(halves, 0))
    return results


def make_per_device(ring):

    def per_device(band_strip, conv_weight, gdn_gamma, gdn_beta, cotangent):
        in_local = band_strip.shape[0]
        row_count = band_strip.shape[1]
        col_count = band_strip.shape[2]
        pixels = row_count * col_count
        lat_local = gdn_gamma.shape[0]
        first = lax.axis_index("chan") == 0
        rimmed = extended(band_strip, (("row", 1),), 1)
        columns = tap_columns(rimmed, row_count, col_count)
        shard_piece = lax.all_gather(conv_weight, "row", axis=0, tiled=True)
        flat = shard_piece.reshape(shard_piece.shape[0], 9 * in_local)
        partial_value = jnp.dot(flat, columns, preferred_element_type=jnp.float32)
        pre = chan_scatter_sum(partial_value)
        squares_own = (pre * pre).astype(jnp.bfloat16)
        squares = chan_gather(squares_own)
        norm_value = gdn_beta[:, None] + jnp.dot(
            gdn_gamma, squares, preferred_element_type=jnp.float32
        )
        inverse = lax.rsqrt(norm_value)
        latent = (pre * inverse).astype(jnp.bfloat16)
        upstream = cotangent.reshape(lat_local, pixels).astype(jnp.float32)
        shares = (-0.5 * upstream * pre * inverse * inverse * inverse).astype(jnp.bfloat16)
        gamma_left, gamma_right = (gdn_gamma[:, :lat_local], gdn_gamma[:, lat_local:])
        gamma_mine = jnp.where(first, gamma_left, gamma_right)
        gamma_theirs = lax.ppermute(jnp.where(first, gamma_right, gamma_left), "chan", SWAP)
        gamma_cols = jnp.where(
            first,
            jnp.concatenate([gamma_mine, gamma_theirs], 0),
            jnp.concatenate([gamma_theirs, gamma_mine], 0),
        )
        shares_all = chan_gather(shares)
        back_sum = lax.dot_general(
            gamma_cols, shares_all, (((0,), (0,)), ((), ())), preferred_element_type=jnp.float32
        )
        latent_grad = (upstream * inverse + 2.0 * pre * back_sum).astype(jnp.bfloat16)
        gamma_terms = lax.dot_general(
            shares, squares, (((1,), (1,)), ((), ())), preferred_element_type=jnp.float32
        )
        beta_terms = jnp.sum(shares.astype(jnp.float32), axis=1)
        if len(ring) <= 16:
            gamma_total, beta_total = ring_sum([gamma_terms, beta_terms], ring)
        else:
            gamma_total, beta_total = lax.psum((gamma_terms, beta_terms), "row")
        scale_factor = 1.0 / math.sqrt(pixels * lax.axis_size("row"))
        grad_gamma = gamma_total * scale_factor
        grad_beta = beta_total * scale_factor
        grad_all = chan_gather(latent_grad.reshape(lat_local, row_count, col_count))
        grad_rimmed = extended(grad_all, (("row", 1),), 1)
        grad_padded = jnp.pad(grad_rimmed, ((0, 0), (0, 0), (1, 1)))
        running = jnp.zeros((in_local, pixels), jnp.float32)
        count_rows = shard_piece.shape[0]
        for tap_index, (row_shift, col_shift) in enumerate(TAPS):
            window = grad_padded[
                :,
                1 - row_shift : 1 - row_shift + row_count,
                1 - col_shift : 1 - col_shift + col_count,
            ].reshape(count_rows, pixels)
            running = running + lax.dot_general(
                shard_piece[:, tap_index, :],
                window,
                (((0,), (0,)), ((), ())),
                preferred_element_type=jnp.float32,
            )
        return (
            latent.reshape(lat_local, row_count, col_count),
            running.reshape(in_local, row_count, col_count),
            grad_gamma,
            grad_beta,
        )

    return per_device


def solution(mesh):
    return jax.shard_map(
        make_per_device(ring_order(mesh)),
        mesh=mesh,
        in_specs=(
            P("chan", ("grp", "row"), None),
            P("row", None, "chan"),
            P("chan", None),
            P("chan"),
            P("chan", ("grp", "row"), None),
        ),
        out_specs=(
            P("chan", ("grp", "row"), None),
            P("chan", ("grp", "row"), None),
            P(("grp", "chan"), None),
            P(("grp", "chan")),
        ),
        check_vma=False,
    )
```

profile of v0, /device:TPU:0, one launch (start us, length us, event | category | flops | bytes accessed | tf_op | source)
XLA Modules:
  0.0 275.6 jit_solution(1936061474365692763)
XLA Ops:
  9.1 4.9 %collective-permute-start = (bf16[212,1,128]{2,1,0:T(2,128)(2,1)S(1)}, bf16[212,1,128]{2,1,0:T(2,128)(2,1)S(1)}, u32[]{:S(2)}, u32[]{:S(2)}) collective-permute-start(bf16[212,1,128]{2,1,0:T(2,128)(2,1)S(1)} %get-tuple-element.59), channel_id=1, source_target_pairs={{0,2},{2,4},{4,6},{6,8},{8,10},{10,12},{12,14},{1,3},{3,5},{5,7},{... | collective-permute-start | bytes 162824 | tf_op jit(solution)/shard_map/ppermute | solution.py:18
  16.3 4.3 %collective-permute-done.1 = bf16[212,1,128]{2,1,0:T(2,128)(2,1)S(1)} collective-permute-done((bf16[212,1,128]{2,1,0:T(2,128)(2,1)S(1)}, bf16[212,1,128]{2,1,0:T(2,128)(2,1)S(1)}, u32[]{:S(2)}, u32[]{:S(2)}) %collective-permute-start.1) | collective-permute-done | bytes 54304 | tf_op jit(solution)/shard_map/ppermute | solution.py:19
  20.6 2.1 fusion.40
  25.6 1.6 copy.16
  27.2 57.8 %all-gather.2.cloned.1.call-done = bf16[1024,9,212]{0,2,1:T(8,128)(2,1)} async-done(((bf16[128,9,212]{0,2,1:T(8,128)(2,1)}), bf16[1024,9,212]{0,2,1:T(8,128)(2,1)}) %all-gather.2.cloned.1.call-update) | async-done | bytes 3907600 | tf_op jit(solution)/shard_map/all_gather | solution.py:124
  85.0 5.6 %reshape.111 = bf16[1024,1908]{0,1:T(8,128)(2,1)} reshape(bf16[1024,9,212]{0,2,1:T(8,128)(2,1)} %all-gather.2.cloned.1.call-done) | data formatting | bytes 7815168 | tf_op jit(solution)/shard_map/reshape | solution.py:125
  90.6 5.1 %convolution_bitcast_fusion = f32[1024,512]{0,1:T(8,128)S(1)} fusion(bf16[1908,512]{1,0:T(8,128)(2,1)} %bitcast.291, bf16[1024,1908]{0,1:T(8,128)(2,1)} %reshape.111), kind=kOutput, calls=%fused_computation.16 | convolution fusion | flops 2000683008 | bytes 7958528 | tf_op jit(solution)/shard_map/dot_general | solution.py:126
  112.1 2.4 copy.10
  115.7 1.8 multiply_convert_fusion.1
  121.0 2.2 convert_reduce_fusion
  124.4 2.0 collective-permute-start.37
  126.4 2.1 fusion.62
  131.6 1.5 collective-permute-start.38
  133.1 1.5 collective-permute-done.52
  135.7 1.5 collective-permute-start.39
  139.3 1.5 collective-permute-start.40
  142.9 1.5 collective-permute-start.41
  146.5 1.5 collective-permute-start.42
  150.0 1.5 collective-permute-start.43
  153.6 1.5 collective-permute-start.44
  157.2 1.5 collective-permute-start.45
  171.5 1.5 collective-permute-start.49
  175.4 2.2 collective-permute-done.64
  184.2 2.0 collective-permute-start.24
  186.2 2.9 %collective-permute-done.10 = f32[32,1024]{1,0:T(8,128)S(1)} collective-permute-done((f32[32,1024]{1,0:T(8,128)S(1)}, f32[32,1024]{1,0:T(8,128)S(1)}, u32[]{:S(2)}, u32[]{:S(2)}) %collective-permute-start.10) | collective-permute-done | bytes 131104 | tf_op jit(solution)/shard_map/ppermute | solution.py:96
  189.2 2.0 collective-permute-start.25
  191.2 2.9 %collective-permute-done.11 = f32[32,1024]{1,0:T(8,128)S(1)} collective-permute-done((f32[32,1024]{1,0:T(8,128)S(1)}, f32[32,1024]{1,0:T(8,128)S(1)}, u32[]{:S(2)}, u32[]{:S(2)}) %collective-permute-start.11) | collective-permute-done | bytes 131104 | tf_op jit(solution)/shard_map/ppermute | solution.py:96
  194.3 2.0 collective-permute-start.26
  196.2 2.9 %collective-permute-done.12 = f32[32,1024]{1,0:T(8,128)S(1)} collective-permute-done((f32[32,1024]{1,0:T(8,128)S(1)}, f32[32,1024]{1,0:T(8,128)S(1)}, u32[]{:S(2)}, u32[]{:S(2)}) %collective-permute-start.12) | collective-permute-done | bytes 131104 | tf_op jit(solution)/shard_map/ppermute | solution.py:96
  199.3 2.0 collective-permute-start.27
  201.3 2.7 fusion.32
  204.3 2.0 collective-permute-start.28
  206.3 3.8 %collective-permute-done.14 = f32[32,1024]{1,0:T(8,128)S(1)} collective-permute-done((f32[32,1024]{1,0:T(8,128)S(1)}, f32[32,1024]{1,0:T(8,128)S(1)}, u32[]{:S(2)}, u32[]{:S(2)}) %collective-permute-start.14) | collective-permute-done | bytes 131104 | tf_op jit(solution)/shard_map/ppermute | solution.py:96
  210.5 1.8 collective-permute-start.29
  212.3 2.9 %collective-permute-done.15 = f32[32,1024]{1,0:T(8,128)S(1)} collective-permute-done((f32[32,1024]{1,0:T(8,128)S(1)}, f32[32,1024]{1,0:T(8,128)S(1)}, u32[]{:S(2)}, u32[]{:S(2)}) %collective-permute-start.15) | collective-permute-done | bytes 131104 | tf_op jit(solution)/shard_map/ppermute | solution.py:96
  215.8 1.6 collective-permute-start.30
  217.8 2.4 collective-permute-start.7
  221.5 2.7 collective-permute-start.17
  225.8 6.9 %collective-permute-done.17 = f32[32,1024]{1,0:T(8,128)S(1)} collective-permute-done((f32[32,1024]{1,0:T(8,128)S(1)}, f32[32,1024]{1,0:T(8,128)S(1)}, u32[]{:S(2)}, u32[]{:S(2)}) %collective-permute-start.17) | collective-permute-done | bytes 131104 | tf_op jit(solution)/shard_map/ppermute | solution.py:101
  232.7 2.5 collective-permute-start.18
  242.1 2.0 collective-permute-start.19
  244.3 3.5 %collective-permute-done.19 = f32[32,1024]{1,0:T(8,128)S(1)} collective-permute-done((f32[32,1024]{1,0:T(8,128)S(1)}, f32[32,1024]{1,0:T(8,128)S(1)}, u32[]{:S(2)}, u32[]{:S(2)}) %collective-permute-start.19) | collective-permute-done | bytes 131104 | tf_op jit(solution)/shard_map/ppermute | solution.py:101
  247.8 2.5 collective-permute-start.20
  250.6 3.4 %collective-permute-done.20 = f32[32,1024]{1,0:T(8,128)S(1)} collective-permute-done((f32[32,1024]{1,0:T(8,128)S(1)}, f32[32,1024]{1,0:T(8,128)S(1)}, u32[]{:S(2)}, u32[]{:S(2)}) %collective-permute-start.20) | collective-permute-done | bytes 131104 | tf_op jit(solution)/shard_map/ppermute | solution.py:101
  254.0 1.7 collective-permute-start.21
  256.4 3.1 %collective-permute-done.21 = f32[32,1024]{1,0:T(8,128)S(1)} collective-permute-done((f32[32,1024]{1,0:T(8,128)S(1)}, f32[32,1024]{1,0:T(8,128)S(1)}, u32[]{:S(2)}, u32[]{:S(2)}) %collective-permute-start.21) | collective-permute-done | bytes 131104 | tf_op jit(solution)/shard_map/ppermute | solution.py:101
  261.6 2.8 %collective-permute-done.22 = f32[32,1024]{1,0:T(8,128)S(1)} collective-permute-done((f32[32,1024]{1,0:T(8,128)S(1)}, f32[32,1024]{1,0:T(8,128)S(1)}, u32[]{:S(2)}, u32[]{:S(2)}) %collective-permute-start.22) | collective-permute-done | bytes 131104 | tf_op jit(solution)/shard_map/ppermute | solution.py:101
  267.3 1.5 maximum_multiply_fusion
  (253 shorter events, 75.1 us)
Async XLA Ops:
  7.2 77.8 %all-gather.2.cloned.1.call-start = ((), (), s32[]{:S(2)}) async-start(), calls=%async_computation | async-start | bytes 4478976 | tf_op jit(solution)/shard_map/all_gather | solution.py:124
  9.1 7.2 %collective-permute-start = (bf16[212,1,128]{2,1,0:T(2,128)(2,1)S(1)}, bf16[212,1,128]{2,1,0:T(2,128)(2,1)S(1)}, u32[]{:S(2)}, u32[]{:S(2)}) collective-permute-start(bf16[212,1,128]{2,1,0:T(2,128)(2,1)S(1)} %get-tuple-element.59), channel_id=1, source_target_pairs={{0,2},{2,4},{4,6},{6,8},{8,10},{10,12},{12,14},{1,3},{3,5},{5,7},{... | collective-permute-start | bytes 162824 | tf_op jit(solution)/shard_map/ppermute | solution.py:18
  14.0 6.6 %collective-permute-start.1 = (bf16[212,1,128]{2,1,0:T(2,128)(2,1)S(1)}, bf16[212,1,128]{2,1,0:T(2,128)(2,1)S(1)}, u32[]{:S(2)}, u32[]{:S(2)}) collective-permute-start(bf16[212,1,128]{2,1,0:T(2,128)(2,1)S(1)} %get-tuple-element.60), channel_id=1, source_target_pairs={{2,0},{4,2},{6,4},{8,6},{10,8},{12,10},{14,12},{3,1},{5,3},{7,5},{... | collective-permute-start | bytes 162824 | tf_op jit(solution)/shard_map/ppermute | solution.py:19
  96.8 18.9 %collective-permute-start.2 = (f32[512,512]{0,1:T(8,128)}, f32[512,512]{0,1:T(8,128)}, u32[]{:S(2)}, u32[]{:S(2)}) collective-permute-start(f32[512,512]{0,1:T(8,128)} %slice_select_fusion), channel_id=1, source_target_pairs={{0,1},{1,0},{2,3},{3,2},{4,5},{5,4},{6,7},{7,6},{8,9},{9,8},{10,11... | collective-permute-start | bytes 3145736 | tf_op jit(solution)/shard_map/ppermute | solution.py:52
  100.5 100.8 %collective-permute-start.4 = (bf16[512,512]{0,1:T(8,128)(2,1)}, bf16[512,512]{0,1:T(8,128)(2,1)}, u32[]{:S(2)}, u32[]{:S(2)}) collective-permute-start(bf16[512,512]{0,1:T(8,128)(2,1)} %get-tuple-element.56), channel_id=1, source_target_pairs={{0,1},{1,0},{2,3},{3,2},{4,5},{5,4},{6,7},{7,6},{8,9},{9,8},{10,11... | collective-permute-start | bytes 1572872 | tf_op jit(solution)/shard_map/ppermute | solution.py:139
  124.4 6.6 %collective-permute-start.51 = (f32[32]{0:T(128)S(1)}, f32[32]{0:T(128)S(1)}, u32[]{:S(2)}, u32[]{:S(2)}) collective-permute-start(f32[32]{0:T(128)S(1)} %fusion.78), channel_id=1, source_target_pairs={{2,0},{6,2},{10,6},{14,10},{12,14},{8,12},{4,8},{0,4},{3,1},{7,3},... | collective-permute-start | bytes 392 | tf_op jit(solution)/shard_map/ppermute | solution.py:96
  124.4 7.2 %collective-permute-start.37 = (f32[32]{0:T(128)S(1)}, f32[32]{0:T(128)S(1)}, u32[]{:S(2)}, u32[]{:S(2)}) collective-permute-start(f32[32]{0:T(128)S(1)} %fusion.63), channel_id=1, source_target_pairs={{0,2},{2,6},{6,10},{10,14},{14,12},{12,8},{8,4},{4,0},{1,3},{3,7},... | collective-permute-start | bytes 392 | tf_op jit(solution)/shard_map/ppermute | solution.py:96
  126.4 74.8 %collective-permute-start.5 = (bf16[512,512]{0,1:T(8,128)(2,1)}, bf16[512,512]{0,1:T(8,128)(2,1)}, u32[]{:S(2)}, u32[]{:S(2)}) collective-permute-start(bf16[512,512]{0,1:T(8,128)(2,1)} %get-tuple-element.35), channel_id=1, source_target_pairs={{0,1},{1,0},{2,3},{3,2},{4,5},{5,4},{6,7},{7,6},{8,9},{9,8},{10,11... | collective-permute-start | bytes 1572872 | tf_op jit(solution)/shard_map/ppermute | solution.py:41
  129.5 54.5 %collective-permute-start.9 = (f32[32,1024]{1,0:T(8,128)}, f32[32,1024]{1,0:T(8,128)S(1)}, u32[]{:S(2)}, u32[]{:S(2)}) collective-permute-start(f32[32,1024]{1,0:T(8,128)} %select_bitcast_fusion.1), channel_id=1, source_target_pairs={{0,2},{2,6},{6,10},{10,14},{14,12},{12,8},{8,4},{4,0},{1,3},{3,7},... | collective-permute-start | bytes 393224 | tf_op jit(solution)/shard_map/ppermute | solution.py:96
  131.0 3.6 %collective-permute-start.52 = (f32[32]{0:T(128)S(1)}, f32[32]{0:T(128)S(1)}, u32[]{:S(2)}, u32[]{:S(2)}) collective-permute-start(f32[32]{0:T(128)S(1)} %fusion.80), channel_id=1, source_target_pairs={{2,0},{6,2},{10,6},{14,10},{12,14},{8,12},{4,8},{0,4},{3,1},{7,3},... | collective-permute-start | bytes 392 | tf_op jit(solution)/shard_map/ppermute | solution.py:96
  131.6 4.1 %collective-permute-start.38 = (f32[32]{0:T(128)S(1)}, f32[32]{0:T(128)S(1)}, u32[]{:S(2)}, u32[]{:S(2)}) collective-permute-start(f32[32]{0:T(128)S(1)} %fusion.65), channel_id=1, source_target_pairs={{0,2},{2,6},{6,10},{10,14},{14,12},{12,8},{8,4},{4,0},{1,3},{3,7},... | collective-permute-start | bytes 392 | tf_op jit(solution)/shard_map/ppermute | solution.py:96
  139.3 3.6 %collective-permute-start.40 = (f32[32]{0:T(128)S(1)}, f32[32]{0:T(128)S(1)}, u32[]{:S(2)}, u32[]{:S(2)}) collective-permute-start(f32[32]{0:T(128)S(1)} %fusion.69), channel_id=1, source_target_pairs={{0,2},{2,6},{6,10},{10,14},{14,12},{12,8},{8,4},{4,0},{1,3},{3,7},... | collective-permute-start | bytes 392 | tf_op jit(solution)/shard_map/ppermute | solution.py:96
  141.8 3.6 %collective-permute-start.55 = (f32[32]{0:T(128)S(1)}, f32[32]{0:T(128)S(1)}, u32[]{:S(2)}, u32[]{:S(2)}) collective-permute-start(f32[32]{0:T(128)S(1)} %fusion.86), channel_id=1, source_target_pairs={{2,0},{6,2},{10,6},{14,10},{12,14},{8,12},{4,8},{0,4},{3,1},{7,3},... | collective-permute-start | bytes 392 | tf_op jit(solution)/shard_map/ppermute | solution.py:96
  149.0 3.6 %collective-permute-start.57 = (f32[32]{0:T(128)S(1)}, f32[32]{0:T(128)S(1)}, u32[]{:S(2)}, u32[]{:S(2)}) collective-permute-start(f32[32]{0:T(128)S(1)} %fusion.90), channel_id=1, source_target_pairs={{2,0},{6,2},{10,6},{14,10},{12,14},{8,12},{4,8},{0,4},{3,1},{7,3},... | collective-permute-start | bytes 392 | tf_op jit(solution)/shard_map/ppermute | solution.py:96
  152.5 3.6 %collective-permute-start.58 = (f32[32]{0:T(128)S(1)}, f32[32]{0:T(128)S(1)}, u32[]{:S(2)}, u32[]{:S(2)}) collective-permute-start(f32[32]{0:T(128)S(1)} %fusion.92), channel_id=1, source_target_pairs={{2,0},{6,2},{10,6},{14,10},{12,14},{8,12},{4,8},{0,4},{3,1},{7,3},... | collective-permute-start | bytes 392 | tf_op jit(solution)/shard_map/ppermute | solution.py:101
  153.6 3.6 %collective-permute-start.44 = (f32[32]{0:T(128)S(1)}, f32[32]{0:T(128)S(1)}, u32[]{:S(2)}, u32[]{:S(2)}) collective-permute-start(f32[32]{0:T(128)S(1)} %fusion.77), channel_id=1, source_target_pairs={{0,2},{2,6},{6,10},{10,14},{14,12},{12,8},{8,4},{4,0},{1,3},{3,7},... | collective-permute-start | bytes 392 | tf_op jit(solution)/shard_map/ppermute | solution.py:101
  174.0 3.6 %collective-permute-start.64 = (f32[32]{0:T(128)S(1)}, f32[32]{0:T(128)S(1)}, u32[]{:S(2)}, u32[]{:S(2)}) collective-permute-start(f32[32]{0:T(128)S(1)} %collective-permute-done.63), channel_id=1, source_target_pairs={{2,0},{6,2},{10,6},{14,10},{12,14},{8,12},{4,8},{0,4},{3,1},{7,3},... | collective-permute-start | bytes 392 | tf_op jit(solution)/shard_map/ppermute | solution.py:101
  175.1 9.1 %collective-permute-start.23 = (f32[32,1024]{1,0:T(8,128)S(1)}, f32[32,1024]{1,0:T(8,128)S(1)}, u32[]{:S(2)}, u32[]{:S(2)}) collective-permute-start(f32[32,1024]{1,0:T(8,128)S(1)} %select_bitcast_fusion), channel_id=1, source_target_pairs={{2,0},{6,2},{10,6},{14,10},{12,14},{8,12},{4,8},{0,4},{3,1},{7,3},... | collective-permute-start | bytes 393224 | tf_op jit(solution)/shard_map/ppermute | solution.py:96
  177.5 3.6 %collective-permute-start.50 = (f32[32]{0:T(128)}, f32[32]{0:T(128)}, u32[]{:S(2)}, u32[]{:S(2)}) collective-permute-start(f32[32]{0:T(128)} %collective-permute-done.49), channel_id=1, source_target_pairs={{0,2},{2,6},{6,10},{10,14},{14,12},{12,8},{8,4},{4,0},{1,3},{3,7},... | collective-permute-start | bytes 392 | tf_op jit(solution)/shard_map/ppermute | solution.py:101
  184.0 5.0 %collective-permute-start.10 = (f32[32,1024]{1,0:T(8,128)S(1)}, f32[32,1024]{1,0:T(8,128)S(1)}, u32[]{:S(2)}, u32[]{:S(2)}) collective-permute-start(f32[32,1024]{1,0:T(8,128)S(1)} %bitcast_add_fusion.13), channel_id=1, source_target_pairs={{0,2},{2,6},{6,10},{10,14},{14,12},{12,8},{8,4},{4,0},{1,3},{3,7},... | collective-permute-start | bytes 393224 | tf_op jit(solution)/shard_map/ppermute | solution.py:96
  184.2 5.0 %collective-permute-start.24 = (f32[32,1024]{1,0:T(8,128)S(1)}, f32[32,1024]{1,0:T(8,128)S(1)}, u32[]{:S(2)}, u32[]{:S(2)}) collective-permute-start(f32[32,1024]{1,0:T(8,128)S(1)} %bitcast_add_fusion.6), channel_id=1, source_target_pairs={{2,0},{6,2},{10,6},{14,10},{12,14},{8,12},{4,8},{0,4},{3,1},{7,3},... | collective-permute-start | bytes 393224 | tf_op jit(solution)/shard_map/ppermute | solution.py:96
  189.0 5.0 %collective-permute-start.11 = (f32[32,1024]{1,0:T(8,128)S(1)}, f32[32,1024]{1,0:T(8,128)S(1)}, u32[]{:S(2)}, u32[]{:S(2)}) collective-permute-start(f32[32,1024]{1,0:T(8,128)S(1)} %bitcast_add_fusion.12), channel_id=1, source_target_pairs={{0,2},{2,6},{6,10},{10,14},{14,12},{12,8},{8,4},{4,0},{1,3},{3,7},... | collective-permute-start | bytes 393224 | tf_op jit(solution)/shard_map/ppermute | solution.py:96
  189.2 5.0 %collective-permute-start.25 = (f32[32,1024]{1,0:T(8,128)S(1)}, f32[32,1024]{1,0:T(8,128)S(1)}, u32[]{:S(2)}, u32[]{:S(2)}) collective-permute-start(f32[32,1024]{1,0:T(8,128)S(1)} %bitcast_add_fusion.5), channel_id=1, source_target_pairs={{2,0},{6,2},{10,6},{14,10},{12,14},{8,12},{4,8},{0,4},{3,1},{7,3},... | collective-permute-start | bytes 393224 | tf_op jit(solution)/shard_map/ppermute | solution.py:96
  194.1 5.0 %collective-permute-start.12 = (f32[32,1024]{1,0:T(8,128)S(1)}, f32[32,1024]{1,0:T(8,128)S(1)}, u32[]{:S(2)}, u32[]{:S(2)}) collective-permute-start(f32[32,1024]{1,0:T(8,128)S(1)} %bitcast_add_fusion.11), channel_id=1, source_target_pairs={{0,2},{2,6},{6,10},{10,14},{14,12},{12,8},{8,4},{4,0},{1,3},{3,7},... | collective-permute-start | bytes 393224 | tf_op jit(solution)/shard_map/ppermute | solution.py:96
  194.3 5.0 %collective-permute-start.26 = (f32[32,1024]{1,0:T(8,128)S(1)}, f32[32,1024]{1,0:T(8,128)S(1)}, u32[]{:S(2)}, u32[]{:S(2)}) collective-permute-start(f32[32,1024]{1,0:T(8,128)S(1)} %bitcast_add_fusion.4), channel_id=1, source_target_pairs={{2,0},{6,2},{10,6},{14,10},{12,14},{8,12},{4,8},{0,4},{3,1},{7,3},... | collective-permute-start | bytes 393224 | tf_op jit(solution)/shard_map/ppermute | solution.py:96
  199.1 5.0 %collective-permute-start.13 = (f32[32,1024]{1,0:T(8,128)S(1)}, f32[32,1024]{1,0:T(8,128)S(1)}, u32[]{:S(2)}, u32[]{:S(2)}) collective-permute-start(f32[32,1024]{1,0:T(8,128)S(1)} %bitcast_add_fusion.10), channel_id=1, source_target_pairs={{0,2},{2,6},{6,10},{10,14},{14,12},{12,8},{8,4},{4,0},{1,3},{3,7},... | collective-permute-start | bytes 393224 | tf_op jit(solution)/shard_map/ppermute | solution.py:96
  199.3 5.0 %collective-permute-start.27 = (f32[32,1024]{1,0:T(8,128)S(1)}, f32[32,1024]{1,0:T(8,128)S(1)}, u32[]{:S(2)}, u32[]{:S(2)}) collective-permute-start(f32[32,1024]{1,0:T(8,128)S(1)} %bitcast_add_fusion.3), channel_id=1, source_target_pairs={{2,0},{6,2},{10,6},{14,10},{12,14},{8,12},{4,8},{0,4},{3,1},{7,3},... | collective-permute-start | bytes 393224 | tf_op jit(solution)/shard_map/ppermute | solution.py:96
  204.1 13.3 %collective-permute-start.6 = (bf16[512,4,128]{0,2,1:T(8,128)(2,1)S(1)}, bf16[512,4,128]{0,2,1:T(8,128)(2,1)S(1)}, u32[]{:S(2)}, u32[]{:S(2)}) collective-permute-start(bf16[512,4,128]{0,2,1:T(8,128)(2,1)S(1)} %bitcast.292), channel_id=1, source_target_pairs={{0,1},{1,0},{2,3},{3,2},{4,5},{5,4},{6,7},{7,6},{8,9},{9,8},{10,11... | collective-permute-start | bytes 1572872 | tf_op jit(solution)/shard_map/ppermute | solution.py:41
  204.2 5.9 %collective-permute-start.14 = (f32[32,1024]{1,0:T(8,128)S(1)}, f32[32,1024]{1,0:T(8,128)S(1)}, u32[]{:S(2)}, u32[]{:S(2)}) collective-permute-start(f32[32,1024]{1,0:T(8,128)S(1)} %bitcast_add_fusion.9), channel_id=1, source_target_pairs={{0,2},{2,6},{6,10},{10,14},{14,12},{12,8},{8,4},{4,0},{1,3},{3,7},... | collective-permute-start | bytes 393224 | tf_op jit(solution)/shard_map/ppermute | solution.py:96
  204.3 6.1 %collective-permute-start.28 = (f32[32,1024]{1,0:T(8,128)S(1)}, f32[32,1024]{1,0:T(8,128)S(1)}, u32[]{:S(2)}, u32[]{:S(2)}) collective-permute-start(f32[32,1024]{1,0:T(8,128)S(1)} %bitcast_add_fusion.2), channel_id=1, source_target_pairs={{2,0},{6,2},{10,6},{14,10},{12,14},{8,12},{4,8},{0,4},{3,1},{7,3},... | collective-permute-start | bytes 393224 | tf_op jit(solution)/shard_map/ppermute | solution.py:96
  210.1 5.1 %collective-permute-start.15 = (f32[32,1024]{1,0:T(8,128)S(1)}, f32[32,1024]{1,0:T(8,128)S(1)}, u32[]{:S(2)}, u32[]{:S(2)}) collective-permute-start(f32[32,1024]{1,0:T(8,128)S(1)} %bitcast_add_fusion.8), channel_id=1, source_target_pairs={{0,2},{2,6},{6,10},{10,14},{14,12},{12,8},{8,4},{4,0},{1,3},{3,7},... | collective-permute-start | bytes 393224 | tf_op jit(solution)/shard_map/ppermute | solution.py:96
  210.5 5.3 %collective-permute-start.29 = (f32[32,1024]{1,0:T(8,128)S(1)}, f32[32,1024]{1,0:T(8,128)S(1)}, u32[]{:S(2)}, u32[]{:S(2)}) collective-permute-start(f32[32,1024]{1,0:T(8,128)S(1)} %bitcast_add_fusion.1), channel_id=1, source_target_pairs={{2,0},{6,2},{10,6},{14,10},{12,14},{8,12},{4,8},{0,4},{3,1},{7,3},... | collective-permute-start | bytes 393224 | tf_op jit(solution)/shard_map/ppermute | solution.py:96
  215.2 6.2 %collective-permute-start.16 = (f32[32,1024]{1,0:T(8,128)S(1)}, f32[32,1024]{1,0:T(8,128)S(1)}, u32[]{:S(2)}, u32[]{:S(2)}) collective-permute-start(f32[32,1024]{1,0:T(8,128)S(1)} %get-tuple-element.37), channel_id=1, source_target_pairs={{0,2},{2,6},{6,10},{10,14},{14,12},{12,8},{8,4},{4,0},{1,3},{3,7},... | collective-permute-start | bytes 393224 | tf_op jit(solution)/shard_map/ppermute | solution.py:101
  215.8 8.4 %collective-permute-start.30 = (f32[32,1024]{1,0:T(8,128)S(1)}, f32[32,1024]{1,0:T(8,128)S(1)}, u32[]{:S(2)}, u32[]{:S(2)}) collective-permute-start(f32[32,1024]{1,0:T(8,128)S(1)} %get-tuple-element.39), channel_id=1, source_target_pairs={{2,0},{6,2},{10,6},{14,10},{12,14},{8,12},{4,8},{0,4},{3,1},{7,3},... | collective-permute-start | bytes 393224 | tf_op jit(solution)/shard_map/ppermute | solution.py:101
  217.8 17.5 %collective-permute-start.7 = (bf16[1024,1,128]{0,2,1:T(8,128)(2,1)S(1)}, bf16[1024,1,128]{0,2,1:T(8,128)(2,1)S(1)}, u32[]{:S(2)}, u32[]{:S(2)}) collective-permute-start(bf16[1024,1,128]{0,2,1:T(8,128)(2,1)S(1)} %get-tuple-element.53), channel_id=1, source_target_pairs={{0,2},{2,4},{4,6},{6,8},{8,10},{10,12},{12,14},{1,3},{3,5},{5,7},{... | collective-permute-start | bytes 786440 | tf_op jit(solution)/shard_map/ppermute | solution.py:18
  220.2 15.1 %collective-permute-start.8 = (bf16[1024,1,128]{0,2,1:T(8,128)(2,1)S(1)}, bf16[1024,1,128]{0,2,1:T(8,128)(2,1)S(1)}, u32[]{:S(2)}, u32[]{:S(2)}) collective-permute-start(bf16[1024,1,128]{0,2,1:T(8,128)(2,1)S(1)} %get-tuple-element.54), channel_id=1, source_target_pairs={{2,0},{4,2},{6,4},{8,6},{10,8},{12,10},{14,12},{3,1},{5,3},{7,5},{... | collective-permute-start | bytes 786440 | tf_op jit(solution)/shard_map/ppermute | solution.py:19
  221.5 11.2 %collective-permute-start.17 = (f32[32,1024]{1,0:T(8,128)S(1)}, f32[32,1024]{1,0:T(8,128)S(1)}, u32[]{:S(2)}, u32[]{:S(2)}) collective-permute-start(f32[32,1024]{1,0:T(8,128)S(1)} %collective-permute-done.16), channel_id=1, source_target_pairs={{0,2},{2,6},{6,10},{10,14},{14,12},{12,8},{8,4},{4,0},{1,3},{3,7},... | collective-permute-start | bytes 393224 | tf_op jit(solution)/shard_map/ppermute | solution.py:101
  224.2 11.0 %collective-permute-start.31 = (f32[32,1024]{1,0:T(8,128)S(1)}, f32[32,1024]{1,0:T(8,128)S(1)}, u32[]{:S(2)}, u32[]{:S(2)}) collective-permute-start(f32[32,1024]{1,0:T(8,128)S(1)} %collective-permute-done.30), channel_id=1, source_target_pairs={{2,0},{6,2},{10,6},{14,10},{12,14},{8,12},{4,8},{0,4},{3,1},{7,3},... | collective-permute-start | bytes 393224 | tf_op jit(solution)/shard_map/ppermute | solution.py:101
  232.7 9.4 %collective-permute-start.18 = (f32[32,1024]{1,0:T(8,128)S(1)}, f32[32,1024]{1,0:T(8,128)S(1)}, u32[]{:S(2)}, u32[]{:S(2)}) collective-permute-start(f32[32,1024]{1,0:T(8,128)S(1)} %collective-permute-done.17), channel_id=1, source_target_pairs={{0,2},{2,6},{6,10},{10,14},{14,12},{12,8},{8,4},{4,0},{1,3},{3,7},... | collective-permute-start | bytes 393224 | tf_op jit(solution)/shard_map/ppermute | solution.py:101
  235.2 9.0 %collective-permute-start.32 = (f32[32,1024]{1,0:T(8,128)S(1)}, f32[32,1024]{1,0:T(8,128)S(1)}, u32[]{:S(2)}, u32[]{:S(2)}) collective-permute-start(f32[32,1024]{1,0:T(8,128)S(1)} %collective-permute-done.31), channel_id=1, source_target_pairs={{2,0},{6,2},{10,6},{14,10},{12,14},{8,12},{4,8},{0,4},{3,1},{7,3},... | collective-permute-start | bytes 393224 | tf_op jit(solution)/shard_map/ppermute | solution.py:101
  242.1 5.6 %collective-permute-start.19 = (f32[32,1024]{1,0:T(8,128)S(1)}, f32[32,1024]{1,0:T(8,128)S(1)}, u32[]{:S(2)}, u32[]{:S(2)}) collective-permute-start(f32[32,1024]{1,0:T(8,128)S(1)} %collective-permute-done.18), channel_id=1, source_target_pairs={{0,2},{2,6},{6,10},{10,14},{14,12},{12,8},{8,4},{4,0},{1,3},{3,7},... | collective-permute-start | bytes 393224 | tf_op jit(solution)/shard_map/ppermute | solution.py:101
  244.2 6.4 %collective-permute-start.33 = (f32[32,1024]{1,0:T(8,128)S(1)}, f32[32,1024]{1,0:T(8,128)S(1)}, u32[]{:S(2)}, u32[]{:S(2)}) collective-permute-start(f32[32,1024]{1,0:T(8,128)S(1)} %collective-permute-done.32), channel_id=1, source_target_pairs={{2,0},{6,2},{10,6},{14,10},{12,14},{8,12},{4,8},{0,4},{3,1},{7,3},... | collective-permute-start | bytes 393224 | tf_op jit(solution)/shard_map/ppermute | solution.py:101
  247.8 6.3 %collective-permute-start.20 = (f32[32,1024]{1,0:T(8,128)S(1)}, f32[32,1024]{1,0:T(8,128)S(1)}, u32[]{:S(2)}, u32[]{:S(2)}) collective-permute-start(f32[32,1024]{1,0:T(8,128)S(1)} %collective-permute-done.19), channel_id=1, source_target_pairs={{0,2},{2,6},{6,10},{10,14},{14,12},{12,8},{8,4},{4,0},{1,3},{3,7},... | collective-permute-start | bytes 393224 | tf_op jit(solution)/shard_map/ppermute | solution.py:101
  250.6 5.5 %collective-permute-start.34 = (f32[32,1024]{1,0:T(8,128)S(1)}, f32[32,1024]{1,0:T(8,128)S(1)}, u32[]{:S(2)}, u32[]{:S(2)}) collective-permute-start(f32[32,1024]{1,0:T(8,128)S(1)} %collective-permute-done.33), channel_id=1, source_target_pairs={{2,0},{6,2},{10,6},{14,10},{12,14},{8,12},{4,8},{0,4},{3,1},{7,3},... | collective-permute-start | bytes 393224 | tf_op jit(solution)/shard_map/ppermute | solution.py:101
  254.0 5.4 %collective-permute-start.21 = (f32[32,1024]{1,0:T(8,128)S(1)}, f32[32,1024]{1,0:T(8,128)S(1)}, u32[]{:S(2)}, u32[]{:S(2)}) collective-permute-start(f32[32,1024]{1,0:T(8,128)S(1)} %collective-permute-done.20), channel_id=1, source_target_pairs={{0,2},{2,6},{6,10},{10,14},{14,12},{12,8},{8,4},{4,0},{1,3},{3,7},... | collective-permute-start | bytes 393224 | tf_op jit(solution)/shard_map/ppermute | solution.py:101
  256.1 5.0 %collective-permute-start.35 = (f32[32,1024]{1,0:T(8,128)S(1)}, f32[32,1024]{1,0:T(8,128)S(1)}, u32[]{:S(2)}, u32[]{:S(2)}) collective-permute-start(f32[32,1024]{1,0:T(8,128)S(1)} %collective-permute-done.34), channel_id=1, source_target_pairs={{2,0},{6,2},{10,6},{14,10},{12,14},{8,12},{4,8},{0,4},{3,1},{7,3},... | collective-permute-start | bytes 393224 | tf_op jit(solution)/shard_map/ppermute | solution.py:101
  259.5 5.0 %collective-permute-start.22 = (f32[32,1024]{1,0:T(8,128)S(1)}, f32[32,1024]{1,0:T(8,128)S(1)}, u32[]{:S(2)}, u32[]{:S(2)}) collective-permute-start(f32[32,1024]{1,0:T(8,128)S(1)} %collective-permute-done.21), channel_id=1, source_target_pairs={{0,2},{2,6},{6,10},{10,14},{14,12},{12,8},{8,4},{4,0},{1,3},{3,7},... | collective-permute-start | bytes 393224 | tf_op jit(solution)/shard_map/ppermute | solution.py:101
  261.1 5.0 %collective-permute-start.36 = (f32[32,1024]{1,0:T(8,128)S(1)}, f32[32,1024]{1,0:T(8,128)S(1)}, u32[]{:S(2)}, u32[]{:S(2)}) collective-permute-start(f32[32,1024]{1,0:T(8,128)S(1)} %collective-permute-done.35), channel_id=1, source_target_pairs={{2,0},{6,2},{10,6},{14,10},{12,14},{8,12},{4,8},{0,4},{3,1},{7,3},... | collective-permute-start | bytes 393224 | tf_op jit(solution)/shard_map/ppermute | solution.py:101
  (46 other events, 350.6 us)
Sparse Core Ops, SparseCore 0:
  10.0 74.9 all-gather.1
where the time goes:
time: 276 us
  waiting for transfers between devices  122 us (44%)
  starting transfers between devices  69.1 us (25%)
  between operations  25.5 us (9%)
  local copies, waits for them, and re-layouts  24.9 us (9%)
  other arithmetic  17.1 us (6%)
  matrix products  16.6 us (6%)
    all_gather x1, waiting for transfers between devices, per_device(): shard_piece = lax.all_gather(conv_weight, 'row', axis=0, tiled=True)  57.8 us
    ppermute x28, waiting for transfers between devices, ring_sum(): gathered[part].append(lax.ppermute(gathered[part][-1], 'row', moves[part]))  33.7 us
    ppermute x28, starting transfers between devices, ring_sum(): gathered[part].append(lax.ppermute(gathered[part][-1], 'row', moves[part]))  29.6 us
    ppermute x28, starting transfers between devices, ring_sum(): got = lax.ppermute(carry[part], 'row', moves[part])  28.9 us
    ppermute x28, waiting for transfers between devices, ring_sum(): got = lax.ppermute(carry[part], 'row', moves[part])  25 us
    ppermute x2, starting transfers between devices, extended(): before = lax.ppermute(last, axis, up)  7.28 us
    unnamed x79, local copies, waits for them, and re-layouts  7.24 us
    reshape x1, local copies, waits for them, and re-layouts, per_device(): flat = shard_piece.reshape(shard_piece.shape[0], 9 * in_local)  5.57 us
  transfers between devices with their start and end apart: 66, of which 43 were waited for; matrix products, arithmetic and copies ran while one was open for 16% of the time, Pallas kernels for 0%

commit v1 on v0

--- a/solution.py
+++ b/solution.py
@@ -121,7 +121,18 @@
         first = lax.axis_index("chan") == 0
         rimmed = extended(band_strip, (("row", 1),), 1)
         columns = tap_columns(rimmed, row_count, col_count)
-        shard_piece = lax.all_gather(conv_weight, "row", axis=0, tiled=True)
+        ways = lax.axis_size("row")
+        up_2 = [(d_2, (d_2 + 1) % ways) for d_2 in range(ways)]
+        down_2 = [(d_2, (d_2 - 1) % ways) for d_2 in range(ways)]
+        earlier, later = ([conv_weight], [conv_weight])
+        for _ in range(ways // 2):
+            earlier.append(lax.ppermute(earlier[-1], "row", up_2))
+        for _ in range((ways - 1) // 2):
+            later.append(lax.ppermute(later[-1], "row", down_2))
+        line = jnp.concatenate([*earlier[::-1], *later[1:]], axis=0)
+        shard_piece = jnp.roll(
+            line, (lax.axis_index("row") - ways // 2) * conv_weight.shape[0], axis=0
+        )
         flat = shard_piece.reshape(shard_piece.shape[0], 9 * in_local)
         partial_value = jnp.dot(flat, columns, preferred_element_type=jnp.float32)
         pre = chan_scatter_sum(partial_value)

time: 276 us -> 287 us (1.040)
  starting transfers between devices: 69.1 us -> 98 us
  between operations: 25.5 us -> 12.3 us
  waiting for transfers between devices: 122 us -> 109 us
  local copies, waits for them, and re-layouts: 24.9 us -> 33.5 us
    all_gather x1 -> x0, waiting for transfers between devices: 57.8 us -> none  [per_device(): shard_piece = lax.all_gather(conv_weight, 'row', axis=0, tiled=True)]
    ppermute x0 -> x7, waiting for transfers between devices: none -> 35.9 us  [the longest x4 26.3 us: per_device(): earlier.append(lax.ppermute(earlier[-1], 'row', up_2))]
    ppermute x0 -> x7, starting transfers between devices: none -> 24.1 us  [the longest x3 16.1 us: per_device(): later.append(lax.ppermute(later[-1], 'row', down_2))]
    ppermute x2, waiting for transfers between devices: 0.98 us -> 9.12 us  [extended(): before = lax.ppermute(last, axis, up)]
    unnamed x79 -> x102, local copies, waits for them, and re-layouts: 7.24 us -> 13.2 us
    ppermute x28, waiting for transfers between devices: 33.7 us -> 30.1 us  [ring_sum(): gathered[part].append(lax.ppermute(gathered[part][-1], 'row', moves[part]))]
    ppermute x2, waiting for transfers between devices: 4.34 us -> 7.46 us  [extended(): after = lax.ppermute(leading, axis, down)]
  transfers between devices with their start and end apart: 66 -> 72, of which waited for: 43 -> 49; matrix products, arithmetic and copies ran while one was open for 16% -> 15% of each run, Pallas kernels for 0% -> 0%
where the time goes in v1:
time: 287 us; the launch traced here: 286 us
  waiting for transfers between devices  109 us (38%)
  starting transfers between devices  98 us (34%)
  local copies, waits for them, and re-layouts  33.5 us (12%)
  matrix products  17.2 us (6%)
  other arithmetic  16.4 us (6%)
  between operations  12.3 us (4%)
    ppermute x28, starting transfers between devices, ring_sum(): gathered[part].append(lax.ppermute(gathered[part][-1], 'row', moves[part]))  31.9 us
    ppermute x28, waiting for transfers between devices, ring_sum(): gathered[part].append(lax.ppermute(gathered[part][-1], 'row', moves[part]))  30.1 us
    ppermute x28, starting transfers between devices, ring_sum(): got = lax.ppermute(carry[part], 'row', moves[part])  29.3 us
    ppermute x28, waiting for transfers between devices, ring_sum(): got = lax.ppermute(carry[part], 'row', moves[part])  26.4 us
    ppermute x4, waiting for transfers between devices, per_device(): earlier.append(lax.ppermute(earlier[-1], 'row', up_2))  26.3 us
    ppermute x3, starting transfers between devices, per_device(): later.append(lax.ppermute(later[-1], 'row', down_2))  16.1 us
    unnamed x102, local copies, waits for them, and re-layouts  13.2 us
    ppermute x3, waiting for transfers between devices, per_device(): later.append(lax.ppermute(later[-1], 'row', down_2))  9.58 us
  transfers between devices with their start and end apart: 72, of which 49 were waited for; matrix products, arithmetic and copies ran while one was open for 15% of the time, Pallas kernels for 0%

profile of v1, /device:TPU:0, one launch (start us, length us, event | category | flops | bytes accessed | tf_op | source)
XLA Modules:
  0.0 286.3 jit_solution(2704817336809289584)
XLA Ops:
  0.6 3.0 %collective-permute-start = (bf16[128,9,212]{0,2,1:T(8,128)(2,1)}, bf16[128,9,212]{0,2,1:T(8,128)(2,1)S(1)}, u32[]{:S(2)}, u32[]{:S(2)}) collective-permute-start(bf16[128,9,212]{0,2,1:T(8,128)(2,1)} %param.15), channel_id=1, source_target_pairs={{0,2},{2,4},{4,6},{6,8},{8,10},{10,12},{12,14},{14,0},{1,3},{3,5},... | collective-permute-start | bytes 1465352 | tf_op jit(solution)/shard_map/ppermute | solution.py:129
  6.2 4.6 %collective-permute-start.7 = (bf16[212,1,128]{2,1,0:T(2,128)(2,1)S(1)}, bf16[212,1,128]{2,1,0:T(2,128)(2,1)S(1)}, u32[]{:S(2)}, u32[]{:S(2)}) collective-permute-start(bf16[212,1,128]{2,1,0:T(2,128)(2,1)S(1)} %get-tuple-element.59), channel_id=1, source_target_pairs={{0,2},{2,4},{4,6},{6,8},{8,10},{10,12},{12,14},{1,3},{3,5},{5,7},{... | collective-permute-start | bytes 162824 | tf_op jit(solution)/shard_map/ppermute | solution.py:18
  10.8 2.5 collective-permute-start.4
  13.2 7.5 %collective-permute-done.8 = bf16[212,1,128]{2,1,0:T(2,128)(2,1)S(1)} collective-permute-done((bf16[212,1,128]{2,1,0:T(2,128)(2,1)S(1)}, bf16[212,1,128]{2,1,0:T(2,128)(2,1)S(1)}, u32[]{:S(2)}, u32[]{:S(2)}) %collective-permute-start.8) | collective-permute-done | bytes 54304 | tf_op jit(solution)/shard_map/ppermute | solution.py:19
  20.7 9.1 %collective-permute-done.7 = bf16[212,1,128]{2,1,0:T(2,128)(2,1)S(1)} collective-permute-done((bf16[212,1,128]{2,1,0:T(2,128)(2,1)S(1)}, bf16[212,1,128]{2,1,0:T(2,128)(2,1)S(1)}, u32[]{:S(2)}, u32[]{:S(2)}) %collective-permute-start.7) | collective-permute-done | bytes 54304 | tf_op jit(solution)/shard_map/ppermute | solution.py:18
  29.8 2.1 fusion.43
  31.9 2.5 collective-permute-start.1
  35.0 11.9 %collective-permute-done.1 = bf16[128,9,212]{0,2,1:T(8,128)(2,1)S(1)} collective-permute-done((bf16[128,9,212]{0,2,1:T(8,128)(2,1)S(1)}, bf16[128,9,212]{0,2,1:T(8,128)(2,1)S(1)}, u32[]{:S(2)}, u32[]{:S(2)}) %collective-permute-start.1) | collective-permute-done | bytes 488480 | tf_op jit(solution)/shard_map/ppermute | solution.py:129
  47.5 4.8 %collective-permute-start.5 = (bf16[128,9,212]{0,2,1:T(8,128)(2,1)S(1)}, bf16[128,9,212]{0,2,1:T(8,128)(2,1)S(1)}, u32[]{:S(2)}, u32[]{:S(2)}) collective-permute-start(bf16[128,9,212]{0,2,1:T(8,128)(2,1)S(1)} %collective-permute-done.4), channel_id=1, source_target_pairs={{0,14},{2,0},{4,2},{6,4},{8,6},{10,8},{12,10},{14,12},{1,15},{3,1}... | collective-permute-start | bytes 1465352 | tf_op jit(solution)/shard_map/ppermute | solution.py:131
  52.2 14.5 %collective-permute-done.2 = bf16[128,9,212]{0,2,1:T(8,128)(2,1)S(1)} collective-permute-done((bf16[128,9,212]{0,2,1:T(8,128)(2,1)S(1)}, bf16[128,9,212]{0,2,1:T(8,128)(2,1)S(1)}, u32[]{:S(2)}, u32[]{:S(2)}) %collective-permute-start.2) | collective-permute-done | bytes 488480 | tf_op jit(solution)/shard_map/ppermute | solution.py:129
  66.7 2.5 collective-permute-start.3
  72.4 8.8 %collective-permute-start.6 = (bf16[128,9,212]{0,2,1:T(8,128)(2,1)S(1)}, bf16[128,9,212]{0,2,1:T(8,128)(2,1)S(1)}, u32[]{:S(2)}, u32[]{:S(2)}) collective-permute-start(bf16[128,9,212]{0,2,1:T(8,128)(2,1)S(1)} %collective-permute-done.5), channel_id=1, source_target_pairs={{0,14},{2,0},{4,2},{6,4},{8,6},{10,8},{12,10},{14,12},{1,15},{3,1}... | collective-permute-start | bytes 1465352 | tf_op jit(solution)/shard_map/ppermute | solution.py:131
  82.5 9.6 %collective-permute-done.6 = bf16[128,9,212]{0,2,1:T(8,128)(2,1)S(1)} collective-permute-done((bf16[128,9,212]{0,2,1:T(8,128)(2,1)S(1)}, bf16[128,9,212]{0,2,1:T(8,128)(2,1)S(1)}, u32[]{:S(2)}, u32[]{:S(2)}) %collective-permute-start.6) | collective-permute-done | bytes 488480 | tf_op jit(solution)/shard_map/ppermute | solution.py:131
  93.7 3.2 %copy-done = bf16[2048,9,212]{0,2,1:T(8,128)(2,1)} copy-done((bf16[2048,9,212]{0,2,1:T(8,128)(2,1)}, bf16[2048,9,212]{0,2,1:T(8,128)(2,1)S(1)}, u32[]{:S(2)}) %copy-start) | copy-done | bytes 7815192
  96.9 2.6 constant_dynamic-slice_fusion.16
  99.5 5.5 %reshape.110 = bf16[1024,1908]{0,1:T(8,128)(2,1)} reshape(bf16[1024,9,212]{0,2,1:T(8,128)(2,1)} %constant_dynamic-slice_fusion.16) | data formatting | bytes 7815168 | tf_op jit(solution)/shard_map/reshape | solution.py:136
  105.1 5.1 %fusion.114 = f32[1024,512]{0,1:T(8,128)S(1)} fusion(bf16[1024,1908]{0,1:T(8,128)(2,1)} %reshape.110, bf16[1908,512]{1,0:T(8,128)(2,1)} %bitcast.281), kind=kOutput, calls=%fused_computation.258 | convolution fusion | flops 2000683008 | bytes 7958528 | tf_op jit(solution)/shard_map/dot_general | solution.py:137
  126.7 2.4 copy.10
  129.8 1.8 multiply_convert_fusion.1
  135.0 2.2 convert_reduce_fusion
  138.5 2.1 fusion.61
  199.9 2.3 collective-permute-start.31
  202.3 2.6 collective-permute-done.31
  204.9 2.3 collective-permute-start.32
  207.6 2.3 collective-permute-done.32
  210.0 2.3 collective-permute-start.33
  212.7 3.1 %fusion.35 = bf16[512,512]{0,1:T(8,128)(2,1)S(1)} fusion(f32[512,512]{0,1:T(8,128)} %get-tuple-element.63, f32[512,4,128]{0,2,1:T(8,128)S(1)} %copy-done.6, f32[512,512]{0,1:T(8,128)S(1)} %get-tuple-element.41, bf16[512,512]{0,1:T(8,128)(2,1)} %collective-permute-done.12, bf16[512,512]{0,1:T(8,128)(2,1)} %get-tuple-element.35, pred[]{:T(512)S(6)} %eq.32, ...), kind=kOutput, calls=%fused_computation.56 | convolution fusion | flops 547618816 | bytes 5767169 | tf_op jit(solution)/shard_map/dot_general | solution.py:157
  216.0 2.1 collective-permute-start.34
  218.1 3.8 %collective-permute-done.34 = f32[32,1024]{1,0:T(8,128)S(1)} collective-permute-done((f32[32,1024]{1,0:T(8,128)S(1)}, f32[32,1024]{1,0:T(8,128)S(1)}, u32[]{:S(2)}, u32[]{:S(2)}) %collective-permute-start.34) | collective-permute-done | bytes 131104 | tf_op jit(solution)/shard_map/ppermute | solution.py:96
  221.9 2.1 collective-permute-start.35
  224.1 2.9 %collective-permute-done.35 = f32[32,1024]{1,0:T(8,128)S(1)} collective-permute-done((f32[32,1024]{1,0:T(8,128)S(1)}, f32[32,1024]{1,0:T(8,128)S(1)}, u32[]{:S(2)}, u32[]{:S(2)}) %collective-permute-start.35) | collective-permute-done | bytes 131104 | tf_op jit(solution)/shard_map/ppermute | solution.py:96
  227.0 2.1 collective-permute-start.36
  229.4 2.6 collective-permute-done.36
  232.1 2.1 collective-permute-start.37
  236.1 4.6 %collective-permute-start.14 = (bf16[1024,1,128]{0,2,1:T(8,128)(2,1)S(1)}, bf16[1024,1,128]{0,2,1:T(8,128)(2,1)S(1)}, u32[]{:S(2)}, u32[]{:S(2)}) collective-permute-start(bf16[1024,1,128]{0,2,1:T(8,128)(2,1)S(1)} %get-tuple-element.53), channel_id=1, source_target_pairs={{0,2},{2,4},{4,6},{6,8},{8,10},{10,12},{12,14},{1,3},{3,5},{5,7},{... | collective-permute-start | bytes 786440 | tf_op jit(solution)/shard_map/ppermute | solution.py:18
  241.3 1.9 collective-permute-start.38
  243.4 3.3 %collective-permute-done.38 = f32[32,1024]{1,0:T(8,128)S(1)} collective-permute-done((f32[32,1024]{1,0:T(8,128)S(1)}, f32[32,1024]{1,0:T(8,128)S(1)}, u32[]{:S(2)}, u32[]{:S(2)}) %collective-permute-start.38) | collective-permute-done | bytes 131104 | tf_op jit(solution)/shard_map/ppermute | solution.py:101
  246.7 2.5 collective-permute-start.39
  249.2 1.8 collective-permute-done.24
  251.0 2.5 collective-permute-start.25
  260.5 2.1 collective-permute-start.26
  262.6 2.8 collective-permute-done.40
  265.5 2.0 collective-permute-start.27
  267.5 3.3 %collective-permute-done.41 = f32[32,1024]{1,0:T(8,128)S(1)} collective-permute-done((f32[32,1024]{1,0:T(8,128)S(1)}, f32[32,1024]{1,0:T(8,128)S(1)}, u32[]{:S(2)}, u32[]{:S(2)}) %collective-permute-start.41) | collective-permute-done | bytes 131104 | tf_op jit(solution)/shard_map/ppermute | solution.py:101
  270.9 2.0 collective-permute-start.28
  272.9 4.1 %collective-permute-done.42 = f32[32,1024]{1,0:T(8,128)S(1)} collective-permute-done((f32[32,1024]{1,0:T(8,128)S(1)}, f32[32,1024]{1,0:T(8,128)S(1)}, u32[]{:S(2)}, u32[]{:S(2)}) %collective-permute-start.42) | collective-permute-done | bytes 131104 | tf_op jit(solution)/shard_map/ppermute | solution.py:101
  277.2 1.9 collective-permute-start.29
  279.1 2.8 collective-permute-done.43
  (290 shorter events, 95.6 us)
Async XLA Ops:
  0.6 31.2 %collective-permute-start = (bf16[128,9,212]{0,2,1:T(8,128)(2,1)}, bf16[128,9,212]{0,2,1:T(8,128)(2,1)S(1)}, u32[]{:S(2)}, u32[]{:S(2)}) collective-permute-start(bf16[128,9,212]{0,2,1:T(8,128)(2,1)} %param.15), channel_id=1, source_target_pairs={{0,2},{2,4},{4,6},{6,8},{8,10},{10,12},{12,14},{14,0},{1,3},{3,5},... | collective-permute-start | bytes 1465352 | tf_op jit(solution)/shard_map/ppermute | solution.py:129
  4.9 15.8 %collective-permute-start.8 = (bf16[212,1,128]{2,1,0:T(2,128)(2,1)S(1)}, bf16[212,1,128]{2,1,0:T(2,128)(2,1)S(1)}, u32[]{:S(2)}, u32[]{:S(2)}) collective-permute-start(bf16[212,1,128]{2,1,0:T(2,128)(2,1)S(1)} %get-tuple-element.60), channel_id=1, source_target_pairs={{2,0},{4,2},{6,4},{8,6},{10,8},{12,10},{14,12},{3,1},{5,3},{7,5},{... | collective-permute-start | bytes 162824 | tf_op jit(solution)/shard_map/ppermute | solution.py:19
  6.2 23.6 %collective-permute-start.7 = (bf16[212,1,128]{2,1,0:T(2,128)(2,1)S(1)}, bf16[212,1,128]{2,1,0:T(2,128)(2,1)S(1)}, u32[]{:S(2)}, u32[]{:S(2)}) collective-permute-start(bf16[212,1,128]{2,1,0:T(2,128)(2,1)S(1)} %get-tuple-element.59), channel_id=1, source_target_pairs={{0,2},{2,4},{4,6},{6,8},{8,10},{10,12},{12,14},{1,3},{3,5},{5,7},{... | collective-permute-start | bytes 162824 | tf_op jit(solution)/shard_map/ppermute | solution.py:18
  10.8 36.7 %collective-permute-start.4 = (bf16[128,9,212]{0,2,1:T(8,128)(2,1)}, bf16[128,9,212]{0,2,1:T(8,128)(2,1)S(1)}, u32[]{:S(2)}, u32[]{:S(2)}) collective-permute-start(bf16[128,9,212]{0,2,1:T(8,128)(2,1)} %param.15), channel_id=1, source_target_pairs={{0,14},{2,0},{4,2},{6,4},{8,6},{10,8},{12,10},{14,12},{1,15},{3,1}... | collective-permute-start | bytes 1465352 | tf_op jit(solution)/shard_map/ppermute | solution.py:131
  31.9 15.0 %collective-permute-start.1 = (bf16[128,9,212]{0,2,1:T(8,128)(2,1)S(1)}, bf16[128,9,212]{0,2,1:T(8,128)(2,1)S(1)}, u32[]{:S(2)}, u32[]{:S(2)}) collective-permute-start(bf16[128,9,212]{0,2,1:T(8,128)(2,1)S(1)} %collective-permute-done), channel_id=1, source_target_pairs={{0,2},{2,4},{4,6},{6,8},{8,10},{10,12},{12,14},{14,0},{1,3},{3,5},... | collective-permute-start | bytes 1465352 | tf_op jit(solution)/shard_map/ppermute | solution.py:129
  46.9 19.8 %collective-permute-start.2 = (bf16[128,9,212]{0,2,1:T(8,128)(2,1)S(1)}, bf16[128,9,212]{0,2,1:T(8,128)(2,1)S(1)}, u32[]{:S(2)}, u32[]{:S(2)}) collective-permute-start(bf16[128,9,212]{0,2,1:T(8,128)(2,1)S(1)} %collective-permute-done.1), channel_id=1, source_target_pairs={{0,2},{2,4},{4,6},{6,8},{8,10},{10,12},{12,14},{14,0},{1,3},{3,5},... | collective-permute-start | bytes 1465352 | tf_op jit(solution)/shard_map/ppermute | solution.py:129
  47.5 25.0 %collective-permute-start.5 = (bf16[128,9,212]{0,2,1:T(8,128)(2,1)S(1)}, bf16[128,9,212]{0,2,1:T(8,128)(2,1)S(1)}, u32[]{:S(2)}, u32[]{:S(2)}) collective-permute-start(bf16[128,9,212]{0,2,1:T(8,128)(2,1)S(1)} %collective-permute-done.4), channel_id=1, source_target_pairs={{0,14},{2,0},{4,2},{6,4},{8,6},{10,8},{12,10},{14,12},{1,15},{3,1}... | collective-permute-start | bytes 1465352 | tf_op jit(solution)/shard_map/ppermute | solution.py:131
  66.7 14.6 %collective-permute-start.3 = (bf16[128,9,212]{0,2,1:T(8,128)(2,1)S(1)}, bf16[128,9,212]{0,2,1:T(8,128)(2,1)S(1)}, u32[]{:S(2)}, u32[]{:S(2)}) collective-permute-start(bf16[128,9,212]{0,2,1:T(8,128)(2,1)S(1)} %collective-permute-done.2), channel_id=1, source_target_pairs={{0,2},{2,4},{4,6},{6,8},{8,10},{10,12},{12,14},{14,0},{1,3},{3,5},... | collective-permute-start | bytes 1465352 | tf_op jit(solution)/shard_map/ppermute | solution.py:129
  72.4 19.6 %collective-permute-start.6 = (bf16[128,9,212]{0,2,1:T(8,128)(2,1)S(1)}, bf16[128,9,212]{0,2,1:T(8,128)(2,1)S(1)}, u32[]{:S(2)}, u32[]{:S(2)}) collective-permute-start(bf16[128,9,212]{0,2,1:T(8,128)(2,1)S(1)} %collective-permute-done.5), channel_id=1, source_target_pairs={{0,14},{2,0},{4,2},{6,4},{8,6},{10,8},{12,10},{14,12},{1,15},{3,1}... | collective-permute-start | bytes 1465352 | tf_op jit(solution)/shard_map/ppermute | solution.py:131
  111.4 18.4 %collective-permute-start.9 = (f32[512,512]{0,1:T(8,128)}, f32[512,512]{0,1:T(8,128)}, u32[]{:S(2)}, u32[]{:S(2)}) collective-permute-start(f32[512,512]{0,1:T(8,128)} %slice_select_fusion), channel_id=1, source_target_pairs={{0,1},{1,0},{2,3},{3,2},{4,5},{5,4},{6,7},{7,6},{8,9},{9,8},{10,11... | collective-permute-start | bytes 3145736 | tf_op jit(solution)/shard_map/ppermute | solution.py:52
  115.1 97.6 %collective-permute-start.11 = (bf16[512,512]{0,1:T(8,128)(2,1)}, bf16[512,512]{0,1:T(8,128)(2,1)}, u32[]{:S(2)}, u32[]{:S(2)}) collective-permute-start(bf16[512,512]{0,1:T(8,128)(2,1)} %get-tuple-element.56), channel_id=1, source_target_pairs={{0,1},{1,0},{2,3},{3,2},{4,5},{5,4},{6,7},{7,6},{8,9},{9,8},{10,11... | collective-permute-start | bytes 1572872 | tf_op jit(solution)/shard_map/ppermute | solution.py:150
  138.2 74.5 %collective-permute-start.12 = (bf16[512,512]{0,1:T(8,128)(2,1)}, bf16[512,512]{0,1:T(8,128)(2,1)}, u32[]{:S(2)}, u32[]{:S(2)}) collective-permute-start(bf16[512,512]{0,1:T(8,128)(2,1)} %get-tuple-element.35), channel_id=1, source_target_pairs={{0,1},{1,0},{2,3},{3,2},{4,5},{5,4},{6,7},{7,6},{8,9},{9,8},{10,11... | collective-permute-start | bytes 1572872 | tf_op jit(solution)/shard_map/ppermute | solution.py:41
  140.9 59.0 %collective-permute-start.30 = (f32[32,1024]{1,0:T(8,128)S(1)}, f32[32,1024]{1,0:T(8,128)S(1)}, u32[]{:S(2)}, u32[]{:S(2)}) collective-permute-start(f32[32,1024]{1,0:T(8,128)S(1)} %select_bitcast_fusion), channel_id=1, source_target_pairs={{2,0},{6,2},{10,6},{14,10},{12,14},{8,12},{4,8},{0,4},{3,1},{7,3},... | collective-permute-start | bytes 393224 | tf_op jit(solution)/shard_map/ppermute | solution.py:96
  142.4 4.3 %collective-permute-start.58 = (f32[32]{0:T(128)S(1)}, f32[32]{0:T(128)S(1)}, u32[]{:S(2)}, u32[]{:S(2)}) collective-permute-start(f32[32]{0:T(128)S(1)} %fusion.86), channel_id=1, source_target_pairs={{2,0},{6,2},{10,6},{14,10},{12,14},{8,12},{4,8},{0,4},{3,1},{7,3},... | collective-permute-start | bytes 392 | tf_op jit(solution)/shard_map/ppermute | solution.py:96
  168.1 3.6 %collective-permute-start.65 = (f32[32]{0:T(128)S(1)}, f32[32]{0:T(128)S(1)}, u32[]{:S(2)}, u32[]{:S(2)}) collective-permute-start(f32[32]{0:T(128)S(1)} %fusion.100), channel_id=1, source_target_pairs={{2,0},{6,2},{10,6},{14,10},{12,14},{8,12},{4,8},{0,4},{3,1},{7,3},... | collective-permute-start | bytes 392 | tf_op jit(solution)/shard_map/ppermute | solution.py:101
  169.7 3.6 %collective-permute-start.51 = (f32[32]{0:T(128)S(1)}, f32[32]{0:T(128)S(1)}, u32[]{:S(2)}, u32[]{:S(2)}) collective-permute-start(f32[32]{0:T(128)S(1)} %fusion.85), channel_id=1, source_target_pairs={{0,2},{2,6},{6,10},{10,14},{14,12},{12,8},{8,4},{4,0},{1,3},{3,7},... | collective-permute-start | bytes 392 | tf_op jit(solution)/shard_map/ppermute | solution.py:101
  187.6 3.7 %collective-permute-start.56 = (f32[32]{0:T(128)S(1)}, f32[32]{0:T(128)}, u32[]{:S(2)}, u32[]{:S(2)}) collective-permute-start(f32[32]{0:T(128)S(1)} %collective-permute-done.55), channel_id=1, source_target_pairs={{0,2},{2,6},{6,10},{10,14},{14,12},{12,8},{8,4},{4,0},{1,3},{3,7},... | collective-permute-start | bytes 392 | tf_op jit(solution)/shard_map/ppermute | solution.py:101
  191.3 10.9 %collective-permute-start.16 = (f32[32,1024]{1,0:T(8,128)}, f32[32,1024]{1,0:T(8,128)S(1)}, u32[]{:S(2)}, u32[]{:S(2)}) collective-permute-start(f32[32,1024]{1,0:T(8,128)} %select_bitcast_fusion.1), channel_id=1, source_target_pairs={{0,2},{2,6},{6,10},{10,14},{14,12},{12,8},{8,4},{4,0},{1,3},{3,7},... | collective-permute-start | bytes 393224 | tf_op jit(solution)/shard_map/ppermute | solution.py:96
  193.2 4.0 %collective-permute-start.57 = (f32[32]{0:T(128)}, f32[32]{0:T(128)}, u32[]{:S(2)}, u32[]{:S(2)}) collective-permute-start(f32[32]{0:T(128)} %collective-permute-done.56), channel_id=1, source_target_pairs={{0,2},{2,6},{6,10},{10,14},{14,12},{12,8},{8,4},{4,0},{1,3},{3,7},... | collective-permute-start | bytes 392 | tf_op jit(solution)/shard_map/ppermute | solution.py:101
  199.9 5.0 %collective-permute-start.31 = (f32[32,1024]{1,0:T(8,128)S(1)}, f32[32,1024]{1,0:T(8,128)S(1)}, u32[]{:S(2)}, u32[]{:S(2)}) collective-permute-start(f32[32,1024]{1,0:T(8,128)S(1)} %bitcast_add_fusion.6), channel_id=1, source_target_pairs={{2,0},{6,2},{10,6},{14,10},{12,14},{8,12},{4,8},{0,4},{3,1},{7,3},... | collective-permute-start | bytes 393224 | tf_op jit(solution)/shard_map/ppermute | solution.py:96
  202.2 5.3 %collective-permute-start.17 = (f32[32,1024]{1,0:T(8,128)S(1)}, f32[32,1024]{1,0:T(8,128)S(1)}, u32[]{:S(2)}, u32[]{:S(2)}) collective-permute-start(f32[32,1024]{1,0:T(8,128)S(1)} %bitcast_add_fusion.13), channel_id=1, source_target_pairs={{0,2},{2,6},{6,10},{10,14},{14,12},{12,8},{8,4},{4,0},{1,3},{3,7},... | collective-permute-start | bytes 393224 | tf_op jit(solution)/shard_map/ppermute | solution.py:96
  204.9 5.0 %collective-permute-start.32 = (f32[32,1024]{1,0:T(8,128)S(1)}, f32[32,1024]{1,0:T(8,128)S(1)}, u32[]{:S(2)}, u32[]{:S(2)}) collective-permute-start(f32[32,1024]{1,0:T(8,128)S(1)} %bitcast_add_fusion.5), channel_id=1, source_target_pairs={{2,0},{6,2},{10,6},{14,10},{12,14},{8,12},{4,8},{0,4},{3,1},{7,3},... | collective-permute-start | bytes 393224 | tf_op jit(solution)/shard_map/ppermute | solution.py:96
  207.6 5.0 %collective-permute-start.18 = (f32[32,1024]{1,0:T(8,128)S(1)}, f32[32,1024]{1,0:T(8,128)S(1)}, u32[]{:S(2)}, u32[]{:S(2)}) collective-permute-start(f32[32,1024]{1,0:T(8,128)S(1)} %bitcast_add_fusion.12), channel_id=1, source_target_pairs={{0,2},{2,6},{6,10},{10,14},{14,12},{12,8},{8,4},{4,0},{1,3},{3,7},... | collective-permute-start | bytes 393224 | tf_op jit(solution)/shard_map/ppermute | solution.py:96
  210.0 6.0 %collective-permute-start.33 = (f32[32,1024]{1,0:T(8,128)S(1)}, f32[32,1024]{1,0:T(8,128)S(1)}, u32[]{:S(2)}, u32[]{:S(2)}) collective-permute-start(f32[32,1024]{1,0:T(8,128)S(1)} %bitcast_add_fusion.4), channel_id=1, source_target_pairs={{2,0},{6,2},{10,6},{14,10},{12,14},{8,12},{4,8},{0,4},{3,1},{7,3},... | collective-permute-start | bytes 393224 | tf_op jit(solution)/shard_map/ppermute | solution.py:96
  212.6 5.5 %collective-permute-start.19 = (f32[32,1024]{1,0:T(8,128)S(1)}, f32[32,1024]{1,0:T(8,128)S(1)}, u32[]{:S(2)}, u32[]{:S(2)}) collective-permute-start(f32[32,1024]{1,0:T(8,128)S(1)} %bitcast_add_fusion.11), channel_id=1, source_target_pairs={{0,2},{2,6},{6,10},{10,14},{14,12},{12,8},{8,4},{4,0},{1,3},{3,7},... | collective-permute-start | bytes 393224 | tf_op jit(solution)/shard_map/ppermute | solution.py:96
  215.9 18.6 %collective-permute-start.13 = (bf16[512,4,128]{0,2,1:T(8,128)(2,1)S(1)}, bf16[512,4,128]{0,2,1:T(8,128)(2,1)S(1)}, u32[]{:S(2)}, u32[]{:S(2)}) collective-permute-start(bf16[512,4,128]{0,2,1:T(8,128)(2,1)S(1)} %bitcast.282), channel_id=1, source_target_pairs={{0,1},{1,0},{2,3},{3,2},{4,5},{5,4},{6,7},{7,6},{8,9},{9,8},{10,11... | collective-permute-start | bytes 1572872 | tf_op jit(solution)/shard_map/ppermute | solution.py:41
  216.0 5.9 %collective-permute-start.34 = (f32[32,1024]{1,0:T(8,128)S(1)}, f32[32,1024]{1,0:T(8,128)S(1)}, u32[]{:S(2)}, u32[]{:S(2)}) collective-permute-start(f32[32,1024]{1,0:T(8,128)S(1)} %bitcast_add_fusion.3), channel_id=1, source_target_pairs={{2,0},{6,2},{10,6},{14,10},{12,14},{8,12},{4,8},{0,4},{3,1},{7,3},... | collective-permute-start | bytes 393224 | tf_op jit(solution)/shard_map/ppermute | solution.py:96
  218.1 5.9 %collective-permute-start.20 = (f32[32,1024]{1,0:T(8,128)S(1)}, f32[32,1024]{1,0:T(8,128)S(1)}, u32[]{:S(2)}, u32[]{:S(2)}) collective-permute-start(f32[32,1024]{1,0:T(8,128)S(1)} %bitcast_add_fusion.10), channel_id=1, source_target_pairs={{0,2},{2,6},{6,10},{10,14},{14,12},{12,8},{8,4},{4,0},{1,3},{3,7},... | collective-permute-start | bytes 393224 | tf_op jit(solution)/shard_map/ppermute | solution.py:96
  221.9 5.1 %collective-permute-start.35 = (f32[32,1024]{1,0:T(8,128)S(1)}, f32[32,1024]{1,0:T(8,128)S(1)}, u32[]{:S(2)}, u32[]{:S(2)}) collective-permute-start(f32[32,1024]{1,0:T(8,128)S(1)} %bitcast_add_fusion.2), channel_id=1, source_target_pairs={{2,0},{6,2},{10,6},{14,10},{12,14},{8,12},{4,8},{0,4},{3,1},{7,3},... | collective-permute-start | bytes 393224 | tf_op jit(solution)/shard_map/ppermute | solution.py:96
  224.0 5.1 %collective-permute-start.21 = (f32[32,1024]{1,0:T(8,128)S(1)}, f32[32,1024]{1,0:T(8,128)S(1)}, u32[]{:S(2)}, u32[]{:S(2)}) collective-permute-start(f32[32,1024]{1,0:T(8,128)S(1)} %bitcast_add_fusion.9), channel_id=1, source_target_pairs={{0,2},{2,6},{6,10},{10,14},{14,12},{12,8},{8,4},{4,0},{1,3},{3,7},... | collective-permute-start | bytes 393224 | tf_op jit(solution)/shard_map/ppermute | solution.py:96
  227.0 5.0 %collective-permute-start.36 = (f32[32,1024]{1,0:T(8,128)S(1)}, f32[32,1024]{1,0:T(8,128)S(1)}, u32[]{:S(2)}, u32[]{:S(2)}) collective-permute-start(f32[32,1024]{1,0:T(8,128)S(1)} %bitcast_add_fusion.1), channel_id=1, source_target_pairs={{2,0},{6,2},{10,6},{14,10},{12,14},{8,12},{4,8},{0,4},{3,1},{7,3},... | collective-permute-start | bytes 393224 | tf_op jit(solution)/shard_map/ppermute | solution.py:96
  229.1 5.0 %collective-permute-start.22 = (f32[32,1024]{1,0:T(8,128)S(1)}, f32[32,1024]{1,0:T(8,128)S(1)}, u32[]{:S(2)}, u32[]{:S(2)}) collective-permute-start(f32[32,1024]{1,0:T(8,128)S(1)} %bitcast_add_fusion.8), channel_id=1, source_target_pairs={{0,2},{2,6},{6,10},{10,14},{14,12},{12,8},{8,4},{4,0},{1,3},{3,7},... | collective-permute-start | bytes 393224 | tf_op jit(solution)/shard_map/ppermute | solution.py:96
  232.1 9.2 %collective-permute-start.37 = (f32[32,1024]{1,0:T(8,128)S(1)}, f32[32,1024]{1,0:T(8,128)S(1)}, u32[]{:S(2)}, u32[]{:S(2)}) collective-permute-start(f32[32,1024]{1,0:T(8,128)S(1)} %get-tuple-element.39), channel_id=1, source_target_pairs={{2,0},{6,2},{10,6},{14,10},{12,14},{8,12},{4,8},{0,4},{3,1},{7,3},... | collective-permute-start | bytes 393224 | tf_op jit(solution)/shard_map/ppermute | solution.py:101
  234.2 8.9 %collective-permute-start.23 = (f32[32,1024]{1,0:T(8,128)S(1)}, f32[32,1024]{1,0:T(8,128)S(1)}, u32[]{:S(2)}, u32[]{:S(2)}) collective-permute-start(f32[32,1024]{1,0:T(8,128)S(1)} %get-tuple-element.37), channel_id=1, source_target_pairs={{0,2},{2,6},{6,10},{10,14},{14,12},{12,8},{8,4},{4,0},{1,3},{3,7},... | collective-permute-start | bytes 393224 | tf_op jit(solution)/shard_map/ppermute | solution.py:101
  234.8 18.7 %collective-permute-start.15 = (bf16[1024,1,128]{0,2,1:T(8,128)(2,1)S(1)}, bf16[1024,1,128]{0,2,1:T(8,128)(2,1)S(1)}, u32[]{:S(2)}, u32[]{:S(2)}) collective-permute-start(bf16[1024,1,128]{0,2,1:T(8,128)(2,1)S(1)} %get-tuple-element.54), channel_id=1, source_target_pairs={{2,0},{4,2},{6,4},{8,6},{10,8},{12,10},{14,12},{3,1},{5,3},{7,5},{... | collective-permute-start | bytes 786440 | tf_op jit(solution)/shard_map/ppermute | solution.py:19
  236.1 17.4 %collective-permute-start.14 = (bf16[1024,1,128]{0,2,1:T(8,128)(2,1)S(1)}, bf16[1024,1,128]{0,2,1:T(8,128)(2,1)S(1)}, u32[]{:S(2)}, u32[]{:S(2)}) collective-permute-start(bf16[1024,1,128]{0,2,1:T(8,128)(2,1)S(1)} %get-tuple-element.53), channel_id=1, source_target_pairs={{0,2},{2,4},{4,6},{6,8},{8,10},{10,12},{12,14},{1,3},{3,5},{5,7},{... | collective-permute-start | bytes 786440 | tf_op jit(solution)/shard_map/ppermute | solution.py:18
  241.3 5.4 %collective-permute-start.38 = (f32[32,1024]{1,0:T(8,128)S(1)}, f32[32,1024]{1,0:T(8,128)S(1)}, u32[]{:S(2)}, u32[]{:S(2)}) collective-permute-start(f32[32,1024]{1,0:T(8,128)S(1)} %collective-permute-done.37), channel_id=1, source_target_pairs={{2,0},{6,2},{10,6},{14,10},{12,14},{8,12},{4,8},{0,4},{3,1},{7,3},... | collective-permute-start | bytes 393224 | tf_op jit(solution)/shard_map/ppermute | solution.py:101
  243.1 7.9 %collective-permute-start.24 = (f32[32,1024]{1,0:T(8,128)S(1)}, f32[32,1024]{1,0:T(8,128)S(1)}, u32[]{:S(2)}, u32[]{:S(2)}) collective-permute-start(f32[32,1024]{1,0:T(8,128)S(1)} %collective-permute-done.23), channel_id=1, source_target_pairs={{0,2},{2,6},{6,10},{10,14},{14,12},{12,8},{8,4},{4,0},{1,3},{3,7},... | collective-permute-start | bytes 393224 | tf_op jit(solution)/shard_map/ppermute | solution.py:101
  246.7 13.8 %collective-permute-start.39 = (f32[32,1024]{1,0:T(8,128)S(1)}, f32[32,1024]{1,0:T(8,128)S(1)}, u32[]{:S(2)}, u32[]{:S(2)}) collective-permute-start(f32[32,1024]{1,0:T(8,128)S(1)} %collective-permute-done.38), channel_id=1, source_target_pairs={{2,0},{6,2},{10,6},{14,10},{12,14},{8,12},{4,8},{0,4},{3,1},{7,3},... | collective-permute-start | bytes 393224 | tf_op jit(solution)/shard_map/ppermute | solution.py:101
  251.0 9.5 %collective-permute-start.25 = (f32[32,1024]{1,0:T(8,128)S(1)}, f32[32,1024]{1,0:T(8,128)S(1)}, u32[]{:S(2)}, u32[]{:S(2)}) collective-permute-start(f32[32,1024]{1,0:T(8,128)S(1)} %collective-permute-done.24), channel_id=1, source_target_pairs={{0,2},{2,6},{6,10},{10,14},{14,12},{12,8},{8,4},{4,0},{1,3},{3,7},... | collective-permute-start | bytes 393224 | tf_op jit(solution)/shard_map/ppermute | solution.py:101
  260.4 5.0 %collective-permute-start.40 = (f32[32,1024]{1,0:T(8,128)S(1)}, f32[32,1024]{1,0:T(8,128)S(1)}, u32[]{:S(2)}, u32[]{:S(2)}) collective-permute-start(f32[32,1024]{1,0:T(8,128)S(1)} %collective-permute-done.39), channel_id=1, source_target_pairs={{2,0},{6,2},{10,6},{14,10},{12,14},{8,12},{4,8},{0,4},{3,1},{7,3},... | collective-permute-start | bytes 393224 | tf_op jit(solution)/shard_map/ppermute | solution.py:101
  260.5 5.0 %collective-permute-start.26 = (f32[32,1024]{1,0:T(8,128)S(1)}, f32[32,1024]{1,0:T(8,128)S(1)}, u32[]{:S(2)}, u32[]{:S(2)}) collective-permute-start(f32[32,1024]{1,0:T(8,128)S(1)} %collective-permute-done.25), channel_id=1, source_target_pairs={{0,2},{2,6},{6,10},{10,14},{14,12},{12,8},{8,4},{4,0},{1,3},{3,7},... | collective-permute-start | bytes 393224 | tf_op jit(solution)/shard_map/ppermute | solution.py:101
  265.4 5.4 %collective-permute-start.41 = (f32[32,1024]{1,0:T(8,128)S(1)}, f32[32,1024]{1,0:T(8,128)S(1)}, u32[]{:S(2)}, u32[]{:S(2)}) collective-permute-start(f32[32,1024]{1,0:T(8,128)S(1)} %collective-permute-done.40), channel_id=1, source_target_pairs={{2,0},{6,2},{10,6},{14,10},{12,14},{8,12},{4,8},{0,4},{3,1},{7,3},... | collective-permute-start | bytes 393224 | tf_op jit(solution)/shard_map/ppermute | solution.py:101
  265.5 5.4 %collective-permute-start.27 = (f32[32,1024]{1,0:T(8,128)S(1)}, f32[32,1024]{1,0:T(8,128)S(1)}, u32[]{:S(2)}, u32[]{:S(2)}) collective-permute-start(f32[32,1024]{1,0:T(8,128)S(1)} %collective-permute-done.26), channel_id=1, source_target_pairs={{0,2},{2,6},{6,10},{10,14},{14,12},{12,8},{8,4},{4,0},{1,3},{3,7},... | collective-permute-start | bytes 393224 | tf_op jit(solution)/shard_map/ppermute | solution.py:101
  270.8 6.2 %collective-permute-start.42 = (f32[32,1024]{1,0:T(8,128)S(1)}, f32[32,1024]{1,0:T(8,128)S(1)}, u32[]{:S(2)}, u32[]{:S(2)}) collective-permute-start(f32[32,1024]{1,0:T(8,128)S(1)} %collective-permute-done.41), channel_id=1, source_target_pairs={{2,0},{6,2},{10,6},{14,10},{12,14},{8,12},{4,8},{0,4},{3,1},{7,3},... | collective-permute-start | bytes 393224 | tf_op jit(solution)/shard_map/ppermute | solution.py:101
  270.9 6.3 %collective-permute-start.28 = (f32[32,1024]{1,0:T(8,128)S(1)}, f32[32,1024]{1,0:T(8,128)S(1)}, u32[]{:S(2)}, u32[]{:S(2)}) collective-permute-start(f32[32,1024]{1,0:T(8,128)S(1)} %collective-permute-done.27), channel_id=1, source_target_pairs={{0,2},{2,6},{6,10},{10,14},{14,12},{12,8},{8,4},{4,0},{1,3},{3,7},... | collective-permute-start | bytes 393224 | tf_op jit(solution)/shard_map/ppermute | solution.py:101
  277.0 5.0 %collective-permute-start.43 = (f32[32,1024]{1,0:T(8,128)S(1)}, f32[32,1024]{1,0:T(8,128)S(1)}, u32[]{:S(2)}, u32[]{:S(2)}) collective-permute-start(f32[32,1024]{1,0:T(8,128)S(1)} %collective-permute-done.42), channel_id=1, source_target_pairs={{2,0},{6,2},{10,6},{14,10},{12,14},{8,12},{4,8},{0,4},{3,1},{7,3},... | collective-permute-start | bytes 393224 | tf_op jit(solution)/shard_map/ppermute | solution.py:101
  277.2 5.8 %collective-permute-start.29 = (f32[32,1024]{1,0:T(8,128)S(1)}, f32[32,1024]{1,0:T(8,128)S(1)}, u32[]{:S(2)}, u32[]{:S(2)}) collective-permute-start(f32[32,1024]{1,0:T(8,128)S(1)} %collective-permute-done.28), channel_id=1, source_target_pairs={{0,2},{2,6},{6,10},{10,14},{14,12},{12,8},{8,4},{4,0},{1,3},{3,7},... | collective-permute-start | bytes 393224 | tf_op jit(solution)/shard_map/ppermute | solution.py:101
  (56 other events, 524.5 us)
